TPU v7x, 32 devices: a whole 2x2x4 slice. The times are simulated.
32 devices in a mesh: grp: 4 (over z), mem: 8 (over y, x, core).
Axes of the slice: x: 2, y: 2, z: 4, core: 2. Of those that a mesh axis runs over, the one named last changes fastest.
Arguments:
- design: bfloat16 [8192, 1024], P(('grp', 'mem'))
- active_blocks: int32 [32, 8], P(('grp', 'mem')), may hold values from 0 to 31, as said below
- ridge: float32 [4096], replicated, may hold values from 0.5 to 2
Outputs:
- factored: float32 [8, 128, 128, 128], P('mem', 'grp')
Inputs may be any that keep to these rules, and one draw needn't show every extreme that they name: active_blocks[d, a] % 8 == a for every device d and position a, so a device's blocks are distinct.
All inputs are finite; a program needn't handle non-finite values.
Results may differ from a plain program's by a relative error of at most 0.0003.
Values sent between devices are 32-bit elements; how exact they have to be, the bound alone decides.
No kernel may reach another device: no remote copies, remote signals or barrier semaphores. Data moves between devices by JAX's collectives and lax.ppermute only.
A program may use at most 64 MiB of HBM per device.

v0:
```python
import jax
import jax.numpy as jnp
from jax import lax
from jax.sharding import PartitionSpec as P

NB = 32
BLK = 128
ACT = 8
HI = lax.Precision.HIGHEST


def panel_solve(column):
    count = column.shape[0]
    chol = jnp.linalg.cholesky(column[0])
    stacked = jnp.transpose(column, (2, 0, 1)).reshape(BLK, count * BLK)
    solved = lax.linalg.triangular_solve(chol, stacked, left_side=True, lower=True)
    lower_col = jnp.transpose(solved.reshape(BLK, count, BLK), (1, 2, 0))
    return lower_col.at[0].set(chol)


def apply_step(tiles, lower_col, step, tile_rows, tile_cols):
    left_tiles = jnp.take(lower_col, jnp.maximum(tile_rows - step, 0), axis=0)
    right_tiles = jnp.take(lower_col, jnp.maximum(tile_cols - step, 0), axis=0)
    update = jnp.einsum("tpr,tqr->tpq", left_tiles, right_tiles, precision=HI)
    trailing = ((tile_rows > step) & (tile_cols > step))[:, None, None]
    on_column = ((tile_cols == step) & (tile_rows >= step))[:, None, None]
    on_row = ((tile_rows == step) & (tile_cols > step))[:, None, None]
    tiles = jnp.where(trailing, tiles - update, tiles)
    tiles = jnp.where(on_column, left_tiles, tiles)
    tiles = jnp.where(on_row, jnp.transpose(right_tiles, (0, 2, 1)), tiles)
    return tiles


def column_picker(step, tile_rows, tile_cols):
    wanted = step + jnp.arange(NB - step, dtype=jnp.int32)
    inside = (tile_cols == step) & (tile_rows >= step)
    return ((tile_rows[None, :] == wanted[:, None]) & inside[None, :]).astype(jnp.float32)


def on_device_general(design, active_blocks, ridge):
    n_mem = lax.axis_size("mem")
    n_grp = lax.axis_size("grp")
    member = lax.axis_index("mem")
    group = lax.axis_index("grp")
    classes = n_mem // 8
    per_pos = ACT // classes
    per_row = NB // ACT
    slot_count = NB // classes * per_row
    owned_count = slot_count // n_grp
    row_count = design.shape[0]
    residue = member // 8
    position = member % 8
    everyone = lax.all_gather(active_blocks, "mem", axis=0, tiled=True)
    blocks = design.reshape(row_count, ACT, BLK)
    left = blocks.reshape(row_count, per_pos, classes, BLK)
    outgoing = jnp.einsum("ncqk,nbl->qbckl", left, blocks, preferred_element_type=jnp.float32)
    outgoing = outgoing.reshape(n_mem, per_pos, BLK, BLK)
    received = lax.all_to_all(outgoing, "mem", split_axis=0, concat_axis=0, tiled=True)
    row_ids = jnp.take(everyone.reshape(n_mem, per_pos, classes), residue, axis=2)
    col_ids = jnp.take(everyone, position, axis=1)
    targets = row_ids // classes * per_row + (col_ids // 8)[:, None]
    onehot = (
        targets.reshape(-1)[None, :] == jnp.arange(slot_count, dtype=jnp.int32)[:, None]
    ).astype(jnp.float32)
    sums = jnp.dot(
        onehot,
        received.reshape(n_mem * per_pos, BLK * BLK),
        precision=HI,
        preferred_element_type=jnp.float32,
    )
    sums = sums.reshape(slot_count, BLK, BLK)
    owned = lax.psum_scatter(sums, "grp", scatter_dimension=0, tiled=True)
    slots = group * owned_count + jnp.arange(owned_count, dtype=jnp.int32)
    tile_rows = slots // per_row * classes + residue
    tile_cols = slots % per_row * 8 + position
    ridge_blocks = jnp.take(ridge.reshape(NB, BLK), tile_rows, axis=0)
    same = (tile_rows == tile_cols).astype(jnp.float32)
    extra = jnp.eye(BLK, dtype=jnp.float32)[None] * ridge_blocks[:, None, :] * same[:, None, None]
    divisor = jnp.float32(row_count * n_grp * n_mem // 16)
    tiles = owned / divisor + extra
    picker = column_picker(0, tile_rows, tile_cols)
    partial_value = jnp.einsum("it,tpq->ipq", picker, tiles, precision=HI)
    column = lax.psum(partial_value, ("grp", "mem"))
    lower_col = panel_solve(column)
    tiles = apply_step(tiles, lower_col, 0, tile_rows, tile_cols)
    return tiles[None]


def on_device_fast(design, active_blocks, ridge):
    n_mem = lax.axis_size("mem")
    n_grp = lax.axis_size("grp")
    member = lax.axis_index("mem")
    group = lax.axis_index("grp")
    per_row = NB // ACT
    row_count = design.shape[0]
    divisor = jnp.float32(row_count * n_grp * n_mem // 16)
    eye = jnp.eye(BLK, dtype=jnp.float32)
    ridge_blocks = ridge.reshape(NB, BLK)
    everyone = lax.all_gather(active_blocks, "mem", axis=0, tiled=True)
    blocks = design.reshape(row_count, ACT, BLK)
    outgoing = jnp.einsum("nak,nbl->bakl", blocks, blocks, preferred_element_type=jnp.float32)
    mine00 = jnp.where(active_blocks[0, 0] == 0, outgoing[0, 0], 0.0)
    gram00 = lax.psum(mine00, ("grp", "mem"))
    a00 = gram00 / divisor + eye * ridge_blocks[0][None, :]
    chol = jnp.linalg.cholesky(a00)
    chol_inv = lax.linalg.triangular_solve(chol, eye, left_side=True, lower=True)
    received = lax.all_to_all(outgoing, "mem", split_axis=0, concat_axis=0, tiled=True)
    received = received.reshape(n_mem, ACT, BLK, BLK)
    row_grp = everyone // 8
    col_grp = jnp.take(everyone, member, axis=1) // 8
    grp_ids = jnp.arange(n_grp, dtype=jnp.int32)
    q_ids = jnp.arange(per_row, dtype=jnp.int32)
    mask = (
        (row_grp[:, :, None, None] == grp_ids[None, None, :, None])
        & (col_grp[:, None, None, None] == q_ids[None, None, None, :])
    ).astype(jnp.float32)
    main = jnp.einsum("sagq,sakl->gaqkl", mask, received, precision=HI)
    main = main.reshape(n_grp, ACT * per_row, BLK, BLK)
    col_mask = ((col_grp[:, None] == grp_ids[None, :]) & (everyone[:, 0:1] == 0)).astype(
        jnp.float32
    )
    col_part = jnp.einsum("sg,slk->gkl", col_mask, received[:, 0], precision=HI)
    send = jnp.concatenate([main, col_part[:, None]], axis=1)
    send = send.reshape(n_grp * (ACT * per_row + 1), BLK, BLK)
    got = lax.psum_scatter(send, "grp", scatter_dimension=0, tiled=True)
    owned = got[: ACT * per_row]
    col_tile = got[ACT * per_row] / divisor
    t = jnp.arange(ACT * per_row, dtype=jnp.int32)
    tile_rows = group * 8 + t // per_row
    tile_cols = t % per_row * 8 + member
    same = (tile_rows == tile_cols).astype(jnp.float32)
    diag = eye[None] * jnp.take(ridge_blocks, tile_rows, axis=0)[:, None, :] * same[:, None, None]
    tiles = owned / divisor + diag
    col_rows = lax.all_gather(col_tile, "mem", axis=0, tiled=False)
    col_cols = lax.all_gather(col_tile, "grp", axis=0, tiled=False)
    p_rows = jnp.einsum("ipr,qr->ipq", col_rows, chol_inv, precision=HI)
    p_cols = jnp.einsum("ipr,qr->ipq", col_cols, chol_inv, precision=HI)
    row_ids = group * 8 + jnp.arange(8, dtype=jnp.int32)
    col_ids = jnp.arange(per_row, dtype=jnp.int32) * 8 + member
    p_rows = jnp.where((row_ids == 0)[:, None, None], chol[None], p_rows)
    p_cols = jnp.where((col_ids == 0)[:, None, None], chol[None], p_cols)
    update = jnp.einsum("apr,qsr->aqps", p_rows, p_cols, precision=HI)
    update = update.reshape(ACT * per_row, BLK, BLK)
    left_tiles = jnp.repeat(p_rows, per_row, axis=0)
    right_tiles = jnp.tile(p_cols, (ACT, 1, 1))
    trailing = ((tile_rows > 0) & (tile_cols > 0))[:, None, None]
    on_column = (tile_cols == 0)[:, None, None]
    on_row = ((tile_rows == 0) & (tile_cols > 0))[:, None, None]
    tiles = jnp.where(trailing, tiles - update, tiles)
    tiles = jnp.where(on_column, left_tiles, tiles)
    tiles = jnp.where(on_row, jnp.transpose(right_tiles, (0, 2, 1)), tiles)
    return tiles[None]


def solution(mesh):
    n_mem = mesh.shape["mem"]
    n_grp = mesh.shape["grp"]
    fast = n_mem == 8 and n_grp * 8 == NB
    body = on_device_fast if fast else on_device_general
    in_specs = (P(("grp", "mem"), None), P(("grp", "mem"), None), P())
    out_specs = P("mem", "grp", None, None)
    return jax.shard_map(body, mesh=mesh, in_specs=in_specs, out_specs=out_specs, check_vma=False)
```

profile of v0, /device:TPU:0, one launch (start us, length us, event | category | flops | bytes accessed | tf_op | source)
XLA Modules:
  0.0 329.3 jit_solution(12028579138386191531)
XLA Ops:
  7.4 1.1 copy.56
  8.5 3.8 %convolution_bitcast_fusion.1 = f32[8,8,128,128]{3,2,1,0:T(8,128)} fusion(bf16[256,8,128,1]{2,1,0,3:T(8,128)(2,1)S(1)} %bitcast.82, bf16[256,1024]{1,0:T(8,128)(2,1)} %param.3), kind=kOutput, calls=%fused_computation.5 | convolution fusion | flops 536870912 | bytes 5242880 | tf_op jit(solution)/shard_map/nak,nbl->bakl/dot_general | solution.py:101
  12.3 5.3 %all-to-all-start = ((f32[8,8,128,128]{3,2,1,0:T(8,128)}), f32[8,8,128,128]{3,2,1,0:T(8,128)}, u32[]{:S(2)}, u32[]{:S(2)}) async-start(f32[8,8,128,128]{3,2,1,0:T(8,128)} %convolution_bitcast_fusion.1), calls=%async_computation | async-start | bytes 8388608 | tf_op jit(solution)/shard_map/all_to_all | solution.py:107
  17.7 1.5 fusion.10
  19.2 50.7 %all-gather = s32[8,1,8]{2,1,0:T(1,128)S(1)} all-gather(s32[1,1,8]{2,1,0:T(1,128)S(1)} %bitcast.87), channel_id=1, replica_groups=mesh['grp'=4,'mem'=8] {'mem'}, dimensions={0}, use_global_device_ids=true | all-gather | bytes 288 | tf_op jit(solution)/shard_map/all_gather | solution.py:99
  70.5 1.1 slice_bitcast_fusion
  71.6 0.7 convolution_bitcast_fusion.3
  72.4 14.0 %convolution_bitcast_fusion = f32[4,8,4,128,128]{4,2,0,3,1:T(4,128)S(1)} fusion(f32[8,8,128,128,1]{3,2,1,0,4:T(8,128)} %bitcast.6, pred[8,4]{0,1:T(4,128)(4,1)S(1)} %iota_compare_fusion.4, pred[8,8,4]{0,2,1:T(4,128)(4,1)S(1)} %iota_compare_fusion.3), kind=kOutput, calls=%fused_computation.2 | convolution fusion | flops 201327616 | bytes 12583200 | tf_op jit(solution)/shard_map/sagq,sakl->gaqkl/dot_general | solution.py:117
  86.4 2.7 copy.41
  89.1 3.9 %pad_maximum_fusion = f32[4,33,128,128]{3,2,1,0:T(8,128)} fusion(f32[4,1,128,128]{3,2,1,0:T(8,128)S(1)} %copy.43, f32[4,32,128,128]{3,2,1,0:T(8,128)S(1)} %bitcast.80), kind=kLoop, calls=%fused_computation.1 | loop fusion | flops 2162688 | bytes 17301504 | tf_op jit(solution)/shard_map/concatenate | solution.py:123
  93.1 0.7 copy-done
  94.5 167.3 %all-reduce.2.cloned.1.call-done = f32[128,128]{1,0:T(8,128)} async-done(((f32[128,128]{1,0:T(8,128)}), f32[128,128]{1,0:T(8,128)}) %all-reduce.2.cloned.1.call-update) | async-done | bytes 65552 | tf_op jit(solution)/shard_map/psum | solution.py:103
  261.8 0.9 select_add_fusion
  262.8 0.9 fusion.12
  263.7 11.7 %cholesky.23 = f32[128,128]{1,0:T(8,128)S(1)} custom-call(f32[128,128]{1,0:T(8,128)S(1)} %fusion.12), custom_call_target="Cholesky" | custom-call | tf_op jit(solution)/shard_map/jit(cholesky)/cholesky | solution.py:105
  275.4 0.6 compare_reduce_fusion
  276.1 0.7 select_bitcast_fusion
  276.7 9.8 %custom-call.6 = f32[1,128,128]{1,2,0:T(8,128)S(1)} custom-call(f32[1,128,128]{2,1,0:T(8,128)S(1)} %get-tuple-element.16), custom_call_target="InvertDiagBlocksLowerTriangular" | custom-call | tf_op jit(solution)/shard_map/triangular_solve | solution.py:106
  286.8 0.8 slice_multiply_fusion.1
  287.7 15.1 %all_gather.12 = f32[4,128,128]{2,1,0:T(8,128)S(1)} all-gather(f32[1,128,128]{2,1,0:T(8,128)S(1)} %slice_multiply_fusion.1), channel_id=1, replica_groups=mesh['grp'=4,'mem'=8] {'grp'}, dimensions={0}, use_global_device_ids=true | all-gather | bytes 327680 | tf_op jit(solution)/shard_map/all_gather | solution.py:135
  302.8 10.0 %all_gather.13 = f32[8,128,128]{2,1,0:T(8,128)S(1)} all-gather(f32[1,128,128]{2,1,0:T(8,128)S(1)} %slice_multiply_fusion.1), channel_id=1, replica_groups=mesh['grp'=4,'mem'=8] {'mem'}, dimensions={0}, use_global_device_ids=true | all-gather | bytes 589824 | tf_op jit(solution)/shard_map/all_gather | solution.py:134
  313.9 1.8 convolution_bitcast_fusion.2
  315.7 1.9 copy.45
  317.6 4.3 %fusion.3 = f32[1,32,128,128]{3,2,1,0:T(8,128)} fusion(f32[33,128,128]{2,1,0:T(8,128)} %reduce-scatter.2.cloned.1.call-done, f32[8,4,128,128]{3,2,1,0:T(8,128)} %copy.45, f32[32]{0:T(128)S(1)} %get-tuple-element.18, f32[32,128]{1,0:T(8,128)S(1)} %broadcast_select_fusion, f32[128,128]{1,0:T(8,128)S(1)} %fusion.13, ...), kind=kLoop, calls=%fused_computation.8 | loop fusion | flops 4194304 | bytes 7160032 | tf_op jit(solution)/shard_map/broadcast_in_dim | solution.py:152
  (34 shorter events, 3.0 us)
Async XLA Ops:
  12.3 5.3 %copy-start.1 = (s32[1,8]{1,0:T(1,128)S(1)}, s32[1,8]{1,0:T(1,128)}, u32[]{:S(2)}) copy-start(s32[1,8]{1,0:T(1,128)} %param.4) | copy-start | bytes 100
  12.3 58.2 %all-to-all-start = ((f32[8,8,128,128]{3,2,1,0:T(8,128)}), f32[8,8,128,128]{3,2,1,0:T(8,128)}, u32[]{:S(2)}, u32[]{:S(2)}) async-start(f32[8,8,128,128]{3,2,1,0:T(8,128)} %convolution_bitcast_fusion.1), calls=%async_computation | async-start | bytes 8388608 | tf_op jit(solution)/shard_map/all_to_all | solution.py:107
  17.6 244.3 %all-reduce.2.cloned.1.call-start = ((), (), s32[]{:S(2)}) async-start(), calls=%async_computation.2 | async-start | bytes 131072 | tf_op jit(solution)/shard_map/psum | solution.py:103
  19.2 267.6 %reduce-scatter.2.cloned.1.call-start = ((), (), s32[]{:S(2)}) async-start(), calls=%async_computation.3 | async-start | bytes 10813440 | tf_op jit(solution)/shard_map/reduce_scatter | solution.py:125
  93.0 0.7 copy-start
Sparse Core Ops, SparseCore 0:
  24.0 237.8 all-reduce.1
Sparse Core Ops, SparseCore 1:
  93.1 149.5 reduce-scatter.1
where the time goes:
time: 330 us; the launch traced here: 329 us
  waiting for transfers between devices  167 us (51%)
  blocking collectives  75.8 us (23%)
  other arithmetic  35.7 us (11%)
  matrix products  21.5 us (7%)
  between operations  15.1 us (5%)
  local copies, waits for them, and re-layouts  8.48 us (3%)
  starting transfers between devices  5.37 us (2%)
    psum x1, waiting for transfers between devices, on_device_fast(): gram00 = lax.psum(mine00, ('grp', 'mem'))  167 us
    all_gather x1, blocking collectives, on_device_fast(): everyone = lax.all_gather(active_blocks, 'mem', axis=0, tiled=True)  50.7 us
    all_gather x1, blocking collectives, on_device_fast(): col_cols = lax.all_gather(col_tile, 'grp', axis=0, tiled=False)  15.1 us
    dot_general x1, matrix products, on_device_fast(): main = jnp.einsum('sagq,sakl->gaqkl', mask, received, precision=HI)  14 us
    another operation x3, other arithmetic, on_device_fast(): chol = jnp.linalg.cholesky(a00)  12.4 us
    another operation x2, other arithmetic, on_device_fast(): lax.linalg.triangular_solve(chol, eye, left_side=True, lower=True)  10.5 us
    all_gather x1, blocking collectives, on_device_fast(): col_rows = lax.all_gather(col_tile, 'mem', axis=0, tiled=False)  10 us
  transfers between devices with their start and end apart: 3, of which 1 were waited for; matrix products, arithmetic and copies ran while one was open for 15% of the time, Pallas kernels for 0%

commit v1 on v0

--- a/solution.py
+++ b/solution.py
@@ -2,6 +2,7 @@
 import jax.numpy as jnp
 from jax import lax
 from jax.sharding import PartitionSpec as P
+from jax.lax import all_gather
 
 NB = 32
 BLK = 128
@@ -100,7 +101,12 @@
     blocks = design.reshape(row_count, ACT, BLK)
     outgoing = jnp.einsum("nak,nbl->bakl", blocks, blocks, preferred_element_type=jnp.float32)
     mine00 = jnp.where(active_blocks[0, 0] == 0, outgoing[0, 0], 0.0)
-    gram00 = lax.psum(mine00, ("grp", "mem"))
+
+    def shape_stages_all(chunk):
+        local_out = all_gather(chunk, ("grp", "mem"))
+        return jnp.sum(local_out, 0)
+
+    gram00 = shape_stages_all(mine00)
     a00 = gram00 / divisor + eye * ridge_blocks[0][None, :]
     chol = jnp.linalg.cholesky(a00)
     chol_inv = lax.linalg.triangular_solve(chol, eye, left_side=True, lower=True)

time: 330 us -> 287 us (0.87)
  waiting for transfers between devices: 167 us -> 123 us
  local copies, waits for them, and re-layouts: 8.48 us -> 14.9 us
  matrix products: 21.5 us -> 16.4 us
    psum x1 -> x0, waiting for transfers between devices: 167 us -> none  [on_device_fast(): gram00 = lax.psum(mine00, ('grp', 'mem'))]
    reduce_scatter x1, waiting for transfers between devices: 0.03 us -> 123 us  [on_device_fast(): got = lax.psum_scatter(send, 'grp', scatter_dimension=0, tiled=True)]
    all_to_all x0 -> x1, local copies, waits for them, and re-layouts: none -> 5.36 us  [on_device_fast(): lax.all_to_all(outgoing, 'mem', split_axis=0, concat_axis=0, tiled=True)]
    dot_general x1, matrix products: 14 us -> 9.26 us  [on_device_fast(): main = jnp.einsum('sagq,sakl->gaqkl', mask, received, precision=HI)]
  transfers between devices with their start and end apart: 3 -> 3, of which waited for: 1 -> 1; matrix products, arithmetic and copies ran while one was open for 15% -> 18% of each run, Pallas kernels for 0% -> 0%
where the time goes in v1:
time: 287 us
  waiting for transfers between devices  123 us (43%)
  blocking collectives  76.4 us (27%)
  other arithmetic  35.1 us (12%)
  matrix products  16.4 us (6%)
  between operations  15.1 us (5%)
  local copies, waits for them, and re-layouts  14.9 us (5%)
  starting transfers between devices  5.38 us (2%)
    reduce_scatter x1, waiting for transfers between devices, on_device_fast(): got = lax.psum_scatter(send, 'grp', scatter_dimension=0, tiled=True)  123 us
    all_gather x1, blocking collectives, on_device_fast(): everyone = lax.all_gather(active_blocks, 'mem', axis=0, tiled=True)  51.8 us
    all_gather x1, blocking collectives, on_device_fast(): col_cols = lax.all_gather(col_tile, 'grp', axis=0, tiled=False)  14.6 us
    another operation x3, other arithmetic, on_device_fast(): chol = jnp.linalg.cholesky(a00)  12.4 us
    another operation x2, other arithmetic, on_device_fast(): lax.linalg.triangular_solve(chol, eye, left_side=True, lower=True)  10.5 us
    all_gather x1, blocking collectives, on_device_fast(): col_rows = lax.all_gather(col_tile, 'mem', axis=0, tiled=False)  10 us
    dot_general x1, matrix products, on_device_fast(): main = jnp.einsum('sagq,sakl->gaqkl', mask, received, precision=HI)  9.26 us
  transfers between devices with their start and end apart: 3, of which 1 were waited for; matrix products, arithmetic and copies ran while one was open for 18% of the time, Pallas kernels for 0%

profile of v1, /device:TPU:0, one launch (start us, length us, event | category | flops | bytes accessed | tf_op | source)
XLA Modules:
  0.0 286.6 jit_solution(6870392667282310443)
XLA Ops:
  7.4 1.1 copy.65
  8.5 3.8 %convolution_bitcast_fusion.1 = f32[8,8,128,128]{2,3,1,0:T(8,128)} fusion(bf16[256,8,128,1]{2,1,0,3:T(8,128)(2,1)S(1)} %bitcast.84, bf16[256,1024]{1,0:T(8,128)(2,1)} %param.3), kind=kOutput, calls=%fused_computation.4 | convolution fusion | flops 536870912 | bytes 5242880 | tf_op jit(solution)/shard_map/nak,nbl->bakl/dot_general | solution.py:102
  12.3 5.3 %all-to-all-start = ((f32[8,8,128,128]{2,3,1,0:T(8,128)}), f32[8,8,128,128]{2,3,1,0:T(8,128)}, u32[]{:S(2)}, u32[]{:S(2)}) async-start(f32[8,8,128,128]{2,3,1,0:T(8,128)} %convolution_bitcast_fusion.1), calls=%async_computation | async-start | bytes 8388608 | tf_op jit(solution)/shard_map/all_to_all | solution.py:113
  17.7 0.8 slice_select_fusion
  18.5 0.7 copy.46
  19.3 51.8 %all-gather.1 = s32[8,1,8]{2,1,0:T(1,128)S(1)} all-gather(s32[1,1,8]{2,1,0:T(1,128)S(1)} %bitcast.89), channel_id=1, replica_groups=mesh['grp'=4,'mem'=8] {'mem'}, dimensions={0}, use_global_device_ids=true | all-gather | bytes 288 | tf_op jit(solution)/shard_map/all_gather | solution.py:100
  71.7 1.1 slice_bitcast_fusion
  73.5 5.4 %copy.57 = f32[8,8,128,128,1]{3,0,4,2,1:T(8,128)} copy(f32[8,8,128,128,1]{2,3,1,0,4:T(8,128)} %bitcast.5) | data formatting | bytes 8388608 | tf_op jit(solution)/shard_map/all_to_all | solution.py:113
  78.9 9.3 %convolution_bitcast_fusion = f32[4,8,4,128,128]{4,2,0,3,1:T(4,128)S(1)} fusion(f32[8,8,128,128,1]{3,0,4,2,1:T(8,128)} %copy.57, pred[8,4]{0,1:T(4,128)(4,1)S(1)} %iota_compare_fusion.5, pred[8,8,4]{0,2,1:T(4,128)(4,1)S(1)} %iota_compare_fusion.4), kind=kOutput, calls=%fused_computation.2 | convolution fusion | flops 201327616 | bytes 12583200 | tf_op jit(solution)/shard_map/sagq,sakl->gaqkl/dot_general | solution.py:123
  88.1 2.7 copy.51
  90.8 3.9 %pad_maximum_fusion = f32[4,33,128,128]{3,2,1,0:T(8,128)} fusion(f32[4,1,128,128]{3,2,1,0:T(8,128)S(1)} %copy.53, f32[4,32,128,128]{3,2,1,0:T(8,128)S(1)} %bitcast.82), kind=kLoop, calls=%fused_computation.1 | loop fusion | flops 2162688 | bytes 17301504 | tf_op jit(solution)/shard_map/concatenate | solution.py:129
  94.8 0.7 copy-done
  96.2 1.7 reduce_sum.9
  98.2 11.7 %cholesky.23 = f32[128,128]{1,0:T(8,128)S(1)} custom-call(f32[128,128]{1,0:T(8,128)S(1)} %fusion.10), custom_call_target="Cholesky" | custom-call | tf_op jit(solution)/shard_map/jit(cholesky)/cholesky | solution.py:111
  110.0 0.6 compare_reduce_fusion
  110.6 0.7 select_bitcast_fusion
  111.3 9.8 %custom-call.6 = f32[1,128,128]{1,2,0:T(8,128)S(1)} custom-call(f32[1,128,128]{2,1,0:T(8,128)S(1)} %get-tuple-element.16), custom_call_target="InvertDiagBlocksLowerTriangular" | custom-call | tf_op jit(solution)/shard_map/triangular_solve | solution.py:112
  121.4 123.3 %reduce-scatter.2.cloned.1.call-done = f32[33,128,128]{2,1,0:T(8,128)} async-done(((f32[132,128,128]{2,1,0:T(8,128)}), f32[33,128,128]{2,1,0:T(8,128)}) %reduce-scatter.2.cloned.1.call-update) | async-done | bytes 2162704 | tf_op jit(solution)/shard_map/reduce_scatter | solution.py:131
  244.7 0.8 slice_multiply_fusion.1
  245.5 14.6 %all_gather.17 = f32[4,128,128]{2,1,0:T(8,128)S(1)} all-gather(f32[1,128,128]{2,1,0:T(8,128)S(1)} %slice_multiply_fusion.1), channel_id=1, replica_groups=mesh['grp'=4,'mem'=8] {'grp'}, dimensions={0}, use_global_device_ids=true | all-gather | bytes 327680 | tf_op jit(solution)/shard_map/all_gather | solution.py:141
  260.1 10.0 %all_gather.18 = f32[8,128,128]{2,1,0:T(8,128)S(1)} all-gather(f32[1,128,128]{2,1,0:T(8,128)S(1)} %slice_multiply_fusion.1), channel_id=1, replica_groups=mesh['grp'=4,'mem'=8] {'mem'}, dimensions={0}, use_global_device_ids=true | all-gather | bytes 589824 | tf_op jit(solution)/shard_map/all_gather | solution.py:140
  271.2 1.8 convolution_bitcast_fusion.2
  273.0 1.9 copy.55
  274.9 4.3 %fusion.2 = f32[1,32,128,128]{3,2,1,0:T(8,128)} fusion(f32[33,128,128]{2,1,0:T(8,128)} %reduce-scatter.2.cloned.1.call-done, f32[8,4,128,128]{3,2,1,0:T(8,128)} %copy.55, f32[32]{0:T(128)S(1)} %get-tuple-element.18, f32[32,128]{1,0:T(8,128)S(1)} %broadcast_select_fusion, f32[128,128]{1,0:T(8,128)S(1)} %fusion.11, ...), kind=kLoop, calls=%fused_computation.7 | loop fusion | flops 4194304 | bytes 7160032 | tf_op jit(solution)/shard_map/broadcast_in_dim | solution.py:158
  (39 shorter events, 3.7 us)
Async XLA Ops:
  12.3 5.3 %copy-start.1 = (s32[1,8]{1,0:T(1,128)S(1)}, s32[1,8]{1,0:T(1,128)}, u32[]{:S(2)}) copy-start(s32[1,8]{1,0:T(1,128)} %param.4) | copy-start | bytes 100
  12.3 59.4 %all-to-all-start = ((f32[8,8,128,128]{2,3,1,0:T(8,128)}), f32[8,8,128,128]{2,3,1,0:T(8,128)}, u32[]{:S(2)}, u32[]{:S(2)}) async-start(f32[8,8,128,128]{2,3,1,0:T(8,128)} %convolution_bitcast_fusion.1), calls=%async_computation | async-start | bytes 8388608 | tf_op jit(solution)/shard_map/all_to_all | solution.py:113
  17.6 78.7 %all-gather.4.cloned.1.call-start = ((), (), s32[]{:S(2)}) async-start(), calls=%async_computation.3 | async-start | bytes 2162688 | tf_op jit(solution)/shard_map/all_gather | solution.py:106
  19.3 225.4 %reduce-scatter.2.cloned.1.call-start = ((), (), s32[]{:S(2)}) async-start(), calls=%async_computation.2 | async-start | bytes 10813440 | tf_op jit(solution)/shard_map/reduce_scatter | solution.py:131
  94.8 0.7 copy-start
Sparse Core Ops, SparseCore 0:
  21.3 69.3 all-gather.3
Sparse Core Ops, SparseCore 1:
  94.9 149.7 reduce-scatter.1
